TPU v7x, 128 devices: a whole 4x4x4 slice. The times are simulated.
128 devices in a mesh: req: 4 (over z), vocab: 32 (over y, x, core).
Axes of the slice: x: 4, y: 4, z: 4, core: 2. Of those that a mesh axis runs over, the one named last changes fastest.
Arguments:
- hidden: bfloat16 [16, 1536, 2048], P('req', 'vocab'), may hold values from -80 to 80
- norm_gain: float32 [2048], replicated, may hold values from 0.6 to 1.4
- head_weight: bfloat16 [2048, 32000], P(None, 'vocab'), may hold values from -2 to 2
- token_ids: int32 [16, 1536], P('req', 'vocab'), may hold values from 0 to 31999
- lengths: int32 [16], replicated, may hold values from 1 to 1536, 15360 in all
- group_ids: int32 [16], replicated, may hold values from 0 to 3
Outputs:
- logprob: float32 [16, 1536], P('req', 'vocab')
- entropy: float32 [16, 1536], P('req', 'vocab')
- centered: float32 [16], replicated
Inputs may be any that keep to these rules, and one draw needn't show every extreme that they name: The lengths sum to 15360; the longest is 1536.
All inputs are finite; a program needn't handle non-finite values.
Results may differ from a plain program's by a relative error of at most 0.00093.
Values may be sent and summed in bfloat16 or wider, within the bound.
No kernel may reach another device: no remote copies, remote signals or barrier semaphores. Data moves between devices by JAX's collectives and lax.ppermute only.
A program may use at most 128 MiB of HBM per device.

v0:
```python
import jax
import jax.numpy as jnp
from jax import lax
from jax.sharding import PartitionSpec as P

norm_eps = 1e-06
OFFLOAD_FLOATS = 8192


def slice_stats(rows, tokens, weight, offset):
    row_count = rows.shape[0]
    block_len = min(512, row_count)
    columns = jnp.arange(weight.shape[1], dtype=jnp.int32)
    results = []
    for block_start in range(0, row_count, block_len):
        block_rows = rows[block_start : block_start + block_len]
        local_ids = tokens[block_start : block_start + block_len] - offset
        logits = jnp.dot(block_rows, weight, preferred_element_type=jnp.float32)
        row_top = jnp.max(logits, axis=1)
        exps = jnp.exp(logits - row_top[:, None])
        exp_total = jnp.sum(exps, axis=1)
        moment = jnp.sum(exps * logits, axis=1)
        picked = jnp.sum(jnp.where(columns[None, :] == local_ids[:, None], logits, 0.0), axis=1)
        results.append(jnp.stack([row_top, exp_total, moment, picked]))
    return jnp.concatenate(results, axis=1)


def combine(stats):
    maxima, sums, moments, picked = (stats[:, 0], stats[:, 1], stats[:, 2], stats[:, 3])
    row_top = jnp.max(maxima, axis=0)
    rescale = jnp.exp(maxima - row_top[None, :])
    exp_total = jnp.sum(sums * rescale, axis=0)
    moment = jnp.sum(moments * rescale, axis=0)
    token_logit = jnp.sum(picked, axis=0)
    log_total = row_top + jnp.log(exp_total)
    return (token_logit - log_total, log_total - moment / exp_total)


def padded_gather(x, axis_name):
    n = x.shape[0]
    width = max(n, OFFLOAD_FLOATS)
    padded = jnp.zeros((1, width), jnp.float32).at[0, :n].set(x)
    return lax.all_gather(padded, axis_name, axis=0, tiled=True)[:, :n]


def body(hidden, norm_gain, head_weight, token_ids, lengths, group_ids):
    req_dev, pos_dev, model_width = hidden.shape
    vocab_dev = head_weight.shape[1]
    n_vocab = lax.axis_size("vocab")
    n_req = lax.axis_size("req")
    vocab_index = lax.axis_index("vocab")
    req_index = lax.axis_index("req")
    values = hidden.astype(jnp.float32)
    squares = jnp.mean(values * values, axis=-1, keepdims=True)
    normed = (values * lax.rsqrt(squares + norm_eps) * norm_gain).astype(jnp.bfloat16)
    offset = vocab_index * vocab_dev
    tok = padded_gather(token_ids.astype(jnp.float32).reshape(-1), "vocab")
    all_tokens = (
        tok.reshape(n_vocab, req_dev, pos_dev)
        .transpose(1, 0, 2)
        .reshape(req_dev, n_vocab * pos_dev)
    )
    all_tokens = all_tokens.astype(jnp.int32)
    full_len = all_tokens.shape[1]
    own_lengths = lax.dynamic_slice_in_dim(lengths, req_index * req_dev, req_dev)
    positions = jnp.arange(full_len, dtype=jnp.int32)
    logprobs, entropies, seq_parts = ([], [], [])
    for k in range(req_dev):
        rows = lax.all_gather(normed[k], "vocab", axis=0, tiled=True)
        part = slice_stats(rows, all_tokens[k], head_weight, offset)
        stats = padded_gather(part.reshape(-1), "vocab").reshape(n_vocab, 4, full_len)
        raw_logprob, raw_entropy = combine(stats)
        is_live = positions < own_lengths[k]
        logprob = jnp.where(is_live, raw_logprob, 0.0)
        entropy = jnp.where(is_live, raw_entropy, 0.0)
        seq_parts.append(jnp.sum(logprob))
        logprobs.append(lax.dynamic_slice_in_dim(logprob, vocab_index * pos_dev, pos_dev))
        entropies.append(lax.dynamic_slice_in_dim(entropy, vocab_index * pos_dev, pos_dev))
    own_seq = jnp.stack(seq_parts)
    slots = jnp.arange(n_req * req_dev, dtype=jnp.int32) // req_dev
    seq_sum = jnp.where(slots == req_index, jnp.tile(own_seq, n_req), 0.0)
    for shift in range(1, n_req):
        moved = lax.ppermute(own_seq, "req", [(i, (i + shift) % n_req) for i in range(n_req)])
        source = (req_index + n_req - shift) % n_req
        seq_sum = seq_sum + jnp.where(slots == source, jnp.tile(moved, n_req), 0.0)
    same = (group_ids[:, None] == group_ids[None, :]).astype(jnp.float32)
    members = jnp.sum(same, axis=1)
    group_mean = jnp.sum(same * seq_sum[None, :], axis=1) / members
    spread = jnp.sum(same * (seq_sum[None, :] - group_mean[:, None]) ** 2, axis=1) / members
    group_std = jnp.maximum(jnp.sqrt(spread), 1.0)
    centered = (seq_sum - group_mean) / group_std
    return (jnp.stack(logprobs), jnp.stack(entropies), centered)


def solution(mesh):
    return jax.shard_map(
        body,
        mesh=mesh,
        in_specs=(P("req", "vocab", None), P(), P(None, "vocab"), P("req", "vocab"), P(), P()),
        out_specs=(P("req", "vocab"), P("req", "vocab"), P()),
        check_vma=False,
    )
```

profile of v0, /device:TPU:1, one launch (start us, length us, event | category | flops | bytes accessed | tf_op | source)
XLA Modules:
  0.0 461.0 jit_solution(11580479027307848466)
XLA Ops:
  11.3 1.4 fusion.26
  16.3 40.0 %all-gather.27.cloned.1.call-done = f32[32,1,8192]{2,1,0:T(1,128)} async-done(((f32[1,1,8192]{2,1,0:T(1,128)}), f32[32,1,8192]{2,1,0:T(1,128)}) %all-gather.27.cloned.1.call-update) | async-done | bytes 1048592 | tf_op jit(solution)/shard_map/all_gather | solution.py:43
  56.2 1.8 copy.146
  58.4 48.4 %all-gather.21.cloned.1.call-done = bf16[1,1536,2048]{2,1,0:T(8,128)(2,1)} async-done(((bf16[1,48,2048]{2,1,0:T(8,128)(2,1)}), bf16[1,1536,2048]{2,1,0:T(8,128)(2,1)}) %all-gather.21.cloned.1.call-update) | async-done | bytes 6291472 | tf_op jit(solution)/shard_map/all_gather | solution.py:69
  106.8 5.3 %fusion.79 = (f32[512]{0:T(512)S(1)}, f32[512,1000]{0,1:T(8,128)S(1)}) fusion(bf16[2048,1000]{0,1:T(8,128)(2,1)} %param.18, bf16[1,1536,2048]{2,1,0:T(8,128)(2,1)} %all-gather.21.cloned.1.call-done), kind=kOutput, calls=%fused_computation.235 | convolution fusion | flops 2097663488 | bytes 8243200 | tf_op jit(solution)/shard_map/dot_general | solution.py:18
  112.8 2.3 fusion.78
  115.7 2.3 fusion.77
  120.3 36.4 %all-gather.19.cloned.1.call-done = bf16[1,1536,2048]{2,1,0:T(8,128)(2,1)} async-done(((bf16[1,48,2048]{2,1,0:T(8,128)(2,1)}), bf16[1,1536,2048]{2,1,0:T(8,128)(2,1)}) %all-gather.19.cloned.1.call-update) | async-done | bytes 6291472 | tf_op jit(solution)/shard_map/all_gather | solution.py:69
  156.8 5.3 %fusion.81 = (f32[512]{0:T(512)S(1)}, f32[512,1000]{0,1:T(8,128)S(1)}) fusion(bf16[2048,1000]{0,1:T(8,128)(2,1)} %param.18, bf16[1,1536,2048]{2,1,0:T(8,128)(2,1)} %all-gather.19.cloned.1.call-done), kind=kOutput, calls=%fused_computation.237 | convolution fusion | flops 2097663488 | bytes 8243200 | tf_op jit(solution)/shard_map/dot_general | solution.py:18
  162.7 2.3 fusion.80
  165.7 2.3 fusion.82
  170.3 36.2 %all-gather.25.cloned.1.call-done = bf16[1,1536,2048]{2,1,0:T(8,128)(2,1)} async-done(((bf16[1,48,2048]{2,1,0:T(8,128)(2,1)}), bf16[1,1536,2048]{2,1,0:T(8,128)(2,1)}) %all-gather.25.cloned.1.call-update) | async-done | bytes 6291472 | tf_op jit(solution)/shard_map/all_gather | solution.py:69
  206.6 5.3 %fusion.73 = (f32[512]{0:T(512)S(1)}, f32[512,1000]{0,1:T(8,128)S(1)}) fusion(bf16[2048,1000]{0,1:T(8,128)(2,1)} %param.18, bf16[1,1536,2048]{2,1,0:T(8,128)(2,1)} %all-gather.25.cloned.1.call-done), kind=kOutput, calls=%fused_computation.229 | convolution fusion | flops 2097663488 | bytes 8243200 | tf_op jit(solution)/shard_map/dot_general | solution.py:18
  212.5 2.3 fusion.72
  215.5 2.3 fusion.71
  220.2 36.2 %all-gather.23.cloned.1.call-done = bf16[1,1536,2048]{2,1,0:T(8,128)(2,1)} async-done(((bf16[1,48,2048]{2,1,0:T(8,128)(2,1)}), bf16[1,1536,2048]{2,1,0:T(8,128)(2,1)}) %all-gather.23.cloned.1.call-update) | async-done | bytes 6291472 | tf_op jit(solution)/shard_map/all_gather | solution.py:69
  256.4 5.3 %fusion.76 = (f32[512]{0:T(512)S(1)}, f32[512,1000]{0,1:T(8,128)S(1)}) fusion(bf16[2048,1000]{0,1:T(8,128)(2,1)} %param.18, bf16[1,1536,2048]{2,1,0:T(8,128)(2,1)} %all-gather.23.cloned.1.call-done), kind=kOutput, calls=%fused_computation.232 | convolution fusion | flops 2097663488 | bytes 8243200 | tf_op jit(solution)/shard_map/dot_general | solution.py:18
  262.3 2.3 fusion.75
  265.3 2.3 fusion.74
  275.5 24.3 %all-gather.31.cloned.1.call-done = f32[32,1,8192]{2,1,0:T(1,128)} async-done(((f32[1,1,8192]{2,1,0:T(1,128)}), f32[32,1,8192]{2,1,0:T(1,128)}) %all-gather.31.cloned.1.call-update) | async-done | bytes 1048592 | tf_op jit(solution)/shard_map/all_gather | solution.py:43
  299.8 1.8 copy.144
  302.2 41.7 %all-gather.29.cloned.1.call-done = f32[32,1,8192]{2,1,0:T(1,128)} async-done(((f32[1,1,8192]{2,1,0:T(1,128)}), f32[32,1,8192]{2,1,0:T(1,128)}) %all-gather.29.cloned.1.call-update) | async-done | bytes 1048592 | tf_op jit(solution)/shard_map/all_gather | solution.py:43
  343.9 1.8 copy.145
  346.3 41.7 %all-gather.35.cloned.1.call-done = f32[32,1,8192]{2,1,0:T(1,128)} async-done(((f32[1,1,8192]{2,1,0:T(1,128)}), f32[32,1,8192]{2,1,0:T(1,128)}) %all-gather.35.cloned.1.call-update) | async-done | bytes 1048592 | tf_op jit(solution)/shard_map/all_gather | solution.py:43
  388.0 1.8 copy.142
  391.9 2.1 fusion.65
  395.1 37.0 %all-gather.33.cloned.1.call-done = f32[32,1,8192]{2,1,0:T(1,128)} async-done(((f32[1,1,8192]{2,1,0:T(1,128)}), f32[32,1,8192]{2,1,0:T(1,128)}) %all-gather.33.cloned.1.call-update) | async-done | bytes 1048592 | tf_op jit(solution)/shard_map/all_gather | solution.py:43
  432.1 1.8 copy.143
  436.4 2.0 fusion.61
  438.6 1.9 fusion.63
  440.5 2.6 pad_maximum_fusion.2
  444.4 2.6 collective-permute-start.1
  (138 shorter events, 42.8 us)
Async XLA Ops:
  7.2 49.1 %all-gather.27.cloned.1.call-start = ((), (), s32[]{:S(2)}) async-start(), calls=%async_computation.4 | async-start | bytes 1081344 | tf_op jit(solution)/shard_map/all_gather | solution.py:43
  9.9 96.9 %all-gather.21.cloned.1.call-start = ((), (), s32[]{:S(2)}) async-start(), calls=%async_computation.1 | async-start | bytes 6488064 | tf_op jit(solution)/shard_map/all_gather | solution.py:69
  13.7 143.1 %all-gather.19.cloned.1.call-start = ((), (), s32[]{:S(2)}) async-start(), calls=%async_computation | async-start | bytes 6488064 | tf_op jit(solution)/shard_map/all_gather | solution.py:69
  14.4 192.1 %all-gather.25.cloned.1.call-start = ((), (), s32[]{:S(2)}) async-start(), calls=%async_computation.3 | async-start | bytes 6488064 | tf_op jit(solution)/shard_map/all_gather | solution.py:69
  15.0 241.4 %all-gather.23.cloned.1.call-start = ((), (), s32[]{:S(2)}) async-start(), calls=%async_computation.2 | async-start | bytes 6488064 | tf_op jit(solution)/shard_map/all_gather | solution.py:69
  15.6 284.2 %all-gather.31.cloned.1.call-start = ((), (), s32[]{:S(2)}) async-start(), calls=%async_computation.6 | async-start | bytes 1081344 | tf_op jit(solution)/shard_map/all_gather | solution.py:43
  106.8 5.9 %copy-start.11 = (bf16[1,1536,2048]{2,1,0:T(8,128)(2,1)S(1)}, bf16[1,1536,2048]{2,1,0:T(8,128)(2,1)}, u32[]{:S(2)}) copy-start(bf16[1,1536,2048]{2,1,0:T(8,128)(2,1)} %all-gather.21.cloned.1.call-done) | copy-start | bytes 18874372
  106.8 6.0 %copy-start.12 = (bf16[2048,1000]{0,1:T(8,128)(2,1)S(1)}, bf16[2048,1000]{0,1:T(8,128)(2,1)}, u32[]{:S(2)}) copy-start(bf16[2048,1000]{0,1:T(8,128)(2,1)} %param.18) | copy-start | bytes 12288004
  120.1 223.8 %all-gather.29.cloned.1.call-start = ((), (), s32[]{:S(2)}) async-start(), calls=%async_computation.5 | async-start | bytes 1081344 | tf_op jit(solution)/shard_map/all_gather | solution.py:43
  156.8 5.9 %copy-start.10 = (bf16[1,1536,2048]{2,1,0:T(8,128)(2,1)S(1)}, bf16[1,1536,2048]{2,1,0:T(8,128)(2,1)}, u32[]{:S(2)}) copy-start(bf16[1,1536,2048]{2,1,0:T(8,128)(2,1)} %all-gather.19.cloned.1.call-done) | copy-start | bytes 18874372
  156.8 6.0 %copy-start.13 = (bf16[2048,1000]{0,1:T(8,128)(2,1)S(1)}, bf16[2048,1000]{0,1:T(8,128)(2,1)}, u32[]{:S(2)}) copy-start(bf16[2048,1000]{0,1:T(8,128)(2,1)} %param.18) | copy-start | bytes 12288004
  170.1 217.9 %all-gather.35.cloned.1.call-start = ((), (), s32[]{:S(2)}) async-start(), calls=%async_computation.8 | async-start | bytes 1081344 | tf_op jit(solution)/shard_map/all_gather | solution.py:43
  206.6 5.9 %copy-start.9 = (bf16[1,1536,2048]{2,1,0:T(8,128)(2,1)S(1)}, bf16[1,1536,2048]{2,1,0:T(8,128)(2,1)}, u32[]{:S(2)}) copy-start(bf16[1,1536,2048]{2,1,0:T(8,128)(2,1)} %all-gather.25.cloned.1.call-done) | copy-start | bytes 18874372
  206.6 6.0 %copy-start.14 = (bf16[2048,1000]{0,1:T(8,128)(2,1)S(1)}, bf16[2048,1000]{0,1:T(8,128)(2,1)}, u32[]{:S(2)}) copy-start(bf16[2048,1000]{0,1:T(8,128)(2,1)} %param.18) | copy-start | bytes 12288004
  219.9 212.2 %all-gather.33.cloned.1.call-start = ((), (), s32[]{:S(2)}) async-start(), calls=%async_computation.7 | async-start | bytes 1081344 | tf_op jit(solution)/shard_map/all_gather | solution.py:43
  256.4 5.9 %copy-start.8 = (bf16[1,1536,2048]{2,1,0:T(8,128)(2,1)S(1)}, bf16[1,1536,2048]{2,1,0:T(8,128)(2,1)}, u32[]{:S(2)}) copy-start(bf16[1,1536,2048]{2,1,0:T(8,128)(2,1)} %all-gather.23.cloned.1.call-done) | copy-start | bytes 18874372
  256.4 6.0 %copy-start.15 = (bf16[2048,1000]{0,1:T(8,128)(2,1)S(1)}, bf16[2048,1000]{0,1:T(8,128)(2,1)}, u32[]{:S(2)}) copy-start(bf16[2048,1000]{0,1:T(8,128)(2,1)} %param.18) | copy-start | bytes 12288004
  267.7 2.1 copy-start.16
  434.0 1.3 copy-start
  434.6 1.0 copy-start.1
  434.6 1.0 copy-start.2
  434.6 1.8 copy-start.3
  434.6 1.8 copy-start.5
  434.6 1.8 copy-start.6
  434.6 4.0 copy-start.4
  434.6 18.4 %copy-start.7 = (s32[16]{0:T(128)S(1)}, s32[16]{0:T(128)}, u32[]{:S(2)}) copy-start(s32[16]{0:T(128)} %param.21) | copy-start | bytes 196
  443.1 9.6 %collective-permute-start = (f32[4]{0:T(128)S(1)}, f32[4]{0:T(128)S(1)}, u32[]{:S(2)}, u32[]{:S(2)}) collective-permute-start(f32[4]{0:T(128)S(1)} %pad_maximum_fusion.2), channel_id=1, source_target_pairs={{0,32},{32,64},{64,96},{96,0},{1,33},{33,65},{65,97},{97,1},{2,34}... | collective-permute-start | bytes 56 | tf_op jit(solution)/shard_map/ppermute | solution.py:83
  444.4 8.4 %collective-permute-start.1 = (f32[4]{0:T(128)S(1)}, f32[4]{0:T(128)S(1)}, u32[]{:S(2)}, u32[]{:S(2)}) collective-permute-start(f32[4]{0:T(128)S(1)} %pad_maximum_fusion.2), channel_id=1, source_target_pairs={{0,64},{32,96},{64,0},{96,32},{1,65},{33,97},{65,1},{97,33},{2,66}... | collective-permute-start | bytes 56 | tf_op jit(solution)/shard_map/ppermute | solution.py:83
  447.0 5.9 %collective-permute-start.2 = (f32[4]{0:T(128)S(1)}, f32[4]{0:T(128)S(1)}, u32[]{:S(2)}, u32[]{:S(2)}) collective-permute-start(f32[4]{0:T(128)S(1)} %pad_maximum_fusion.2), channel_id=1, source_target_pairs={{0,96},{32,0},{64,32},{96,64},{1,97},{33,1},{65,33},{97,65},{2,98}... | collective-permute-start | bytes 56 | tf_op jit(solution)/shard_map/ppermute | solution.py:83
Sparse Core Ops, SparseCore 0:
  10.2 45.9 all-gather.26
  58.5 48.2 all-gather.20
  109.0 47.6 all-gather.18
  158.9 47.6 all-gather.24
  208.7 47.6 all-gather.22
  258.5 41.2 all-gather.30
  302.0 41.7 all-gather.28
  346.1 41.7 all-gather.34
  390.3 41.8 all-gather.32
where the time goes:
time: 469 us; the launch traced here: 461 us
  waiting for transfers between devices  344 us (73%)
  matrix products  39.6 us (8%)
  other arithmetic  38.9 us (8%)
  local copies, waits for them, and re-layouts  17.9 us (4%)
  between operations  14.9 us (3%)
  starting transfers between devices  5.95 us (1%)
    all_gather x5, waiting for transfers between devices, padded_gather(): return lax.all_gather(padded, axis_name, axis=0, tiled=True)[:, :n]  185 us
    all_gather x4, waiting for transfers between devices, body(): rows = lax.all_gather(normed[k], 'vocab', axis=0, tiled=True)  157 us
    dot_general x12, matrix products, slice_stats(): logits = jnp.dot(block_rows, weight, preferred_element_type=jnp.float32)  39.6 us
    unnamed x48, local copies, waits for them, and re-layouts  12.7 us
  transfers between devices with their start and end apart: 12, of which 9 were waited for; matrix products, arithmetic and copies ran while one was open for 18% of the time, Pallas kernels for 0%

commit v1 on v0

--- a/solution.py
+++ b/solution.py
@@ -66,7 +66,9 @@
     positions = jnp.arange(full_len, dtype=jnp.int32)
     logprobs, entropies, seq_parts = ([], [], [])
     for k in range(req_dev):
-        rows = lax.all_gather(normed[k], "vocab", axis=0, tiled=True)
+        rows = jnp.concatenate(
+            lax.all_to_all(jnp.stack([normed[k]] * lax.axis_size("vocab")), "vocab", 0, 0), axis=0
+        )
         part = slice_stats(rows, all_tokens[k], head_weight, offset)
         stats = padded_gather(part.reshape(-1), "vocab").reshape(n_vocab, 4, full_len)
         raw_logprob, raw_entropy = combine(stats)

time: 469 us -> 491 us (1.047)
  waiting for transfers between devices: 344 us -> 245 us
  blocking collectives: 0 us -> 81.7 us
  starting transfers between devices: 5.95 us -> 28.4 us
  matrix products: 39.6 us -> 50.5 us
  local copies, waits for them, and re-layouts: 17.9 us -> 27.5 us
    all_to_all x0 -> x3, waiting for transfers between devices: none -> 173 us  [body(): lax.all_to_all(jnp.stack([normed[k]] * lax.axis_size('vocab')), 'vocab',...]
    all_gather x4 -> x0, waiting for transfers between devices: 157 us -> none  [body(): rows = lax.all_gather(normed[k], 'vocab', axis=0, tiled=True)]
    all_gather x5, waiting for transfers between devices: 185 us -> 71.9 us  [padded_gather(): return lax.all_gather(padded, axis_name, axis=0, tiled=True)[:, :n]]
    all_to_all x0 -> x1, blocking collectives: none -> 81.7 us  [body(): lax.all_to_all(jnp.stack([normed[k]] * lax.axis_size('vocab')), 'vocab',...]
    all_to_all x0 -> x3, starting transfers between devices: none -> 23.6 us  [body(): lax.all_to_all(jnp.stack([normed[k]] * lax.axis_size('vocab')), 'vocab',...]
    another operation x1 -> x5, local copies, waits for them, and re-layouts: 0.08 us -> 11.1 us  [the longest x4 11 us: body(): jnp.stack([normed[k]] * lax.axis_size('vocab'))]
    dot_general x12, matrix products: 39.6 us -> 50.5 us  [slice_stats(): logits = jnp.dot(block_rows, weight, preferred_element_type=jnp.float32)]
  transfers between devices with their start and end apart: 12 -> 11, of which waited for: 9 -> 5; matrix products, arithmetic and copies ran while one was open for 18% -> 20% of each run, Pallas kernels for 0% -> 0%
where the time goes in v1:
time: 491 us; the launch traced here: 487 us
  waiting for transfers between devices  245 us (50%)
  blocking collectives  81.7 us (17%)
  matrix products  50.5 us (10%)
  other arithmetic  39.6 us (8%)
  starting transfers between devices  28.4 us (6%)
  local copies, waits for them, and re-layouts  27.5 us (6%)
  between operations  14.6 us (3%)
    all_to_all x3, waiting for transfers between devices, body(): lax.all_to_all(jnp.stack([normed[k]] * lax.axis_size('vocab')), 'vocab',...  173 us
    all_to_all x1, blocking collectives, body(): lax.all_to_all(jnp.stack([normed[k]] * lax.axis_size('vocab')), 'vocab',...  81.7 us
    all_gather x5, waiting for transfers between devices, padded_gather(): return lax.all_gather(padded, axis_name, axis=0, tiled=True)[:, :n]  71.9 us
    dot_general x12, matrix products, slice_stats(): logits = jnp.dot(block_rows, weight, preferred_element_type=jnp.float32)  50.5 us
    all_to_all x3, starting transfers between devices, body(): lax.all_to_all(jnp.stack([normed[k]] * lax.axis_size('vocab')), 'vocab',...  23.6 us
    unnamed x48, local copies, waits for them, and re-layouts  12.4 us
    another operation x4, local copies, waits for them, and re-layouts, body(): jnp.stack([normed[k]] * lax.axis_size('vocab'))  11 us
  transfers between devices with their start and end apart: 11, of which 5 were waited for; matrix products, arithmetic and copies ran while one was open for 20% of the time, Pallas kernels for 0%

profile of v1, /device:TPU:1, one launch (start us, length us, event | category | flops | bytes accessed | tf_op | source)
XLA Modules:
  0.0 487.1 jit_solution(15478050465018028685)
XLA Ops:
  10.8 81.7 %all_to_all.20 = bf16[32,48,2048]{2,1,0:T(8,128)(2,1)} all-to-all(bf16[32,48,2048]{2,1,0:T(8,128)(2,1)S(1)} %stack.271), channel_id=1, replica_groups=mesh['req'=4,'vocab'=32] {'vocab'}, dimensions={0} | all-to-all | bytes 12582912 | tf_op jit(solution)/shard_map/all_to_all | solution.py:70
  92.5 3.5 stack.288
  96.0 5.0 %all-to-all-start.3 = ((bf16[32,48,2048]{2,1,0:T(8,128)(2,1)}), bf16[32,48,2048]{2,1,0:T(8,128)(2,1)}, u32[]{:S(2)}, u32[]{:S(2)}) async-start(bf16[32,48,2048]{2,1,0:T(8,128)(2,1)} %stack.288), calls=%async_computation.3 | async-start | bytes 12582912 | tf_op jit(solution)/shard_map/all_to_all | solution.py:70
  103.1 73.1 %all-to-all-done.3 = bf16[32,48,2048]{2,1,0:T(8,128)(2,1)} async-done(((bf16[32,48,2048]{2,1,0:T(8,128)(2,1)}), bf16[32,48,2048]{2,1,0:T(8,128)(2,1)}, u32[]{:S(2)}, u32[]{:S(2)}) %all-to-all-start.3) | async-done | bytes 6291488 | tf_op jit(solution)/shard_map/all_to_all | solution.py:70
  176.2 3.4 stack.237
  179.6 9.6 %all-to-all-start = ((bf16[32,48,2048]{2,1,0:T(8,128)(2,1)}), bf16[32,48,2048]{2,1,0:T(8,128)(2,1)}, u32[]{:S(2)}, u32[]{:S(2)}) async-start(bf16[32,48,2048]{2,1,0:T(8,128)(2,1)} %stack.237), calls=%async_computation | async-start | bytes 12582912 | tf_op jit(solution)/shard_map/all_to_all | solution.py:70
  192.5 5.3 %fusion.85 = (f32[512]{0:T(512)S(1)}, f32[512,1000]{0,1:T(8,128)S(1)}) fusion(bf16[2048,1000]{0,1:T(8,128)(2,1)} %param.18, bf16[1536,2048]{1,0:T(8,128)(2,1)} %bitcast.230), kind=kOutput, calls=%fused_computation.233 | convolution fusion | flops 2097663488 | bytes 8243200 | tf_op jit(solution)/shard_map/dot_general | solution.py:18
  198.5 2.3 fusion.86
  201.5 2.3 fusion.87
  205.8 5.1 %fusion.82 = (f32[512]{0:T(512)S(1)}, f32[512,1000]{0,1:T(8,128)S(1)}) fusion(bf16[2048,1000]{0,1:T(8,128)(2,1)} %param.18, bf16[1536,2048]{1,0:T(8,128)(2,1)} %bitcast.70), kind=kOutput, calls=%fused_computation.230 | convolution fusion | flops 2097663488 | bytes 8243200 | tf_op jit(solution)/shard_map/dot_general | solution.py:18
  210.9 52.6 %all-to-all-done = bf16[32,48,2048]{2,1,0:T(8,128)(2,1)} async-done(((bf16[32,48,2048]{2,1,0:T(8,128)(2,1)}), bf16[32,48,2048]{2,1,0:T(8,128)(2,1)}, u32[]{:S(2)}, u32[]{:S(2)}) %all-to-all-start) | async-done | bytes 6291488 | tf_op jit(solution)/shard_map/all_to_all | solution.py:70
  263.5 3.4 stack.254
  266.9 9.0 %all-to-all-start.1 = ((bf16[32,48,2048]{2,1,0:T(8,128)(2,1)}), bf16[32,48,2048]{2,1,0:T(8,128)(2,1)}, u32[]{:S(2)}, u32[]{:S(2)}) async-start(bf16[32,48,2048]{2,1,0:T(8,128)(2,1)} %stack.254), calls=%async_computation.1 | async-start | bytes 12582912 | tf_op jit(solution)/shard_map/all_to_all | solution.py:70
  276.8 5.3 %fusion.83 = (f32[512]{0:T(512)S(1)}, f32[512,1000]{0,1:T(8,128)S(1)}) fusion(bf16[2048,1000]{0,1:T(8,128)(2,1)} %param.18, bf16[1536,2048]{1,0:T(8,128)(2,1)} %bitcast.70), kind=kOutput, calls=%fused_computation.231 | convolution fusion | flops 2097663488 | bytes 8243200 | tf_op jit(solution)/shard_map/dot_general | solution.py:18
  282.7 3.9 fusion.84
  288.1 3.9 fusion.91
  292.7 3.9 fusion.92
  297.3 3.9 fusion.93
  303.3 47.0 %all-to-all-done.1 = bf16[32,48,2048]{2,1,0:T(8,128)(2,1)} async-done(((bf16[32,48,2048]{2,1,0:T(8,128)(2,1)}), bf16[32,48,2048]{2,1,0:T(8,128)(2,1)}, u32[]{:S(2)}, u32[]{:S(2)}) %all-to-all-start.1) | async-done | bytes 6291488 | tf_op jit(solution)/shard_map/all_to_all | solution.py:70
  350.3 6.6 %fusion.88 = (f32[512]{0:T(512)S(1)}, f32[512,1000]{0,1:T(8,128)}) fusion(bf16[2048,1000]{0,1:T(8,128)(2,1)} %param.18, bf16[1536,2048]{1,0:T(8,128)(2,1)} %bitcast.26), kind=kOutput, calls=%fused_computation.236 | convolution fusion | flops 2097663488 | bytes 8243200 | tf_op jit(solution)/shard_map/dot_general | solution.py:18
  356.9 4.0 fusion.89
  361.8 2.4 fusion.30
  364.9 4.0 fusion.90
  379.0 1.8 copy.142
  381.4 35.5 %all-gather.13.cloned.1.call-done = f32[32,1,8192]{2,1,0:T(1,128)} async-done(((f32[1,1,8192]{2,1,0:T(1,128)}), f32[32,1,8192]{2,1,0:T(1,128)}) %all-gather.13.cloned.1.call-update) | async-done | bytes 1048592 | tf_op jit(solution)/shard_map/all_gather | solution.py:43
  419.3 1.9 fusion.79
  421.2 2.1 fusion.80
  424.4 36.4 %all-gather.15.cloned.1.call-done = f32[32,1,8192]{2,1,0:T(1,128)} async-done(((f32[1,1,8192]{2,1,0:T(1,128)}), f32[32,1,8192]{2,1,0:T(1,128)}) %all-gather.15.cloned.1.call-update) | async-done | bytes 1048592 | tf_op jit(solution)/shard_map/all_gather | solution.py:43
  464.2 1.9 fusion.75
  466.3 2.0 fusion.73
  468.3 2.5 pad_maximum_fusion.2
  470.8 2.7 collective-permute-start.2
  (138 shorter events, 44.5 us)
Async XLA Ops:
  96.0 5.7 %copy-start.9 = (s32[4,48]{1,0:T(4,128)S(1)}, s32[4,48]{1,0:T(4,128)}, u32[]{:S(2)}) copy-start(s32[4,48]{1,0:T(4,128)} %param.19) | copy-start | bytes 2308
  96.0 80.2 %all-to-all-start.3 = ((bf16[32,48,2048]{2,1,0:T(8,128)(2,1)}), bf16[32,48,2048]{2,1,0:T(8,128)(2,1)}, u32[]{:S(2)}, u32[]{:S(2)}) async-start(bf16[32,48,2048]{2,1,0:T(8,128)(2,1)} %stack.288), calls=%async_computation.3 | async-start | bytes 12582912 | tf_op jit(solution)/shard_map/all_to_all | solution.py:70
  101.0 89.4 %all-gather.11.cloned.1.call-start = ((), (), s32[]{:S(2)}) async-start(), calls=%async_computation.4 | async-start | bytes 1081344 | tf_op jit(solution)/shard_map/all_gather | solution.py:43
  179.6 83.9 %all-to-all-start = ((bf16[32,48,2048]{2,1,0:T(8,128)(2,1)}), bf16[32,48,2048]{2,1,0:T(8,128)(2,1)}, u32[]{:S(2)}, u32[]{:S(2)}) async-start(bf16[32,48,2048]{2,1,0:T(8,128)(2,1)} %stack.237), calls=%async_computation | async-start | bytes 12582912 | tf_op jit(solution)/shard_map/all_to_all | solution.py:70
  189.2 187.3 %all-gather.17.cloned.1.call-start = ((), (), s32[]{:S(2)}) async-start(), calls=%async_computation.7 | async-start | bytes 1081344 | tf_op jit(solution)/shard_map/all_gather | solution.py:43
  192.5 6.0 %slice-start = ((s8[6291456]{0:T(1024)(128)(4,1)}), s8[4194304]{0:T(1024)(128)(4,1)S(1)}, s32[]{:S(2)}) async-start(s8[6291456]{0:T(1024)(128)(4,1)} %bitcast.231), calls=%async_computation.9 | async-start | bytes 8388608
  192.5 6.0 %slice-start.1 = ((s8[6291456]{0:T(1024)(128)(4,1)}), s8[2097152]{0:T(1024)(128)(4,1)S(1)}, s32[]{:S(2)}) async-start(s8[6291456]{0:T(1024)(128)(4,1)} %bitcast.231), calls=%async_computation.10 | async-start | bytes 4194304
  192.5 6.0 %copy-start.10 = (bf16[2048,1000]{0,1:T(8,128)(2,1)S(1)}, bf16[2048,1000]{0,1:T(8,128)(2,1)}, u32[]{:S(2)}) copy-start(bf16[2048,1000]{0,1:T(8,128)(2,1)} %param.18) | copy-start | bytes 12288004
  266.9 83.4 %all-to-all-start.1 = ((bf16[32,48,2048]{2,1,0:T(8,128)(2,1)}), bf16[32,48,2048]{2,1,0:T(8,128)(2,1)}, u32[]{:S(2)}, u32[]{:S(2)}) async-start(bf16[32,48,2048]{2,1,0:T(8,128)(2,1)} %stack.254), calls=%async_computation.1 | async-start | bytes 12582912 | tf_op jit(solution)/shard_map/all_to_all | solution.py:70
  275.9 103.1 %all-gather.19.cloned.1.call-start = ((), (), s32[]{:S(2)}) async-start(), calls=%async_computation.8 | async-start | bytes 1081344 | tf_op jit(solution)/shard_map/all_gather | solution.py:43
  276.8 6.0 %copy-start.11 = (bf16[2048,1000]{0,1:T(8,128)(2,1)S(1)}, bf16[2048,1000]{0,1:T(8,128)(2,1)}, u32[]{:S(2)}) copy-start(bf16[2048,1000]{0,1:T(8,128)(2,1)} %param.18) | copy-start | bytes 12288004
  303.3 113.6 %all-gather.13.cloned.1.call-start = ((), (), s32[]{:S(2)}) async-start(), calls=%async_computation.5 | async-start | bytes 1081344 | tf_op jit(solution)/shard_map/all_gather | solution.py:43
  350.3 6.6 %copy-start.12 = (bf16[2048,1000]{0,1:T(8,128)(2,1)S(1)}, bf16[2048,1000]{0,1:T(8,128)(2,1)}, u32[]{:S(2)}) copy-start(bf16[2048,1000]{0,1:T(8,128)(2,1)} %param.18) | copy-start | bytes 12288004
  361.5 99.3 %all-gather.15.cloned.1.call-start = ((), (), s32[]{:S(2)}) async-start(), calls=%async_computation.6 | async-start | bytes 1081344 | tf_op jit(solution)/shard_map/all_gather | solution.py:43
  361.8 3.1 copy-start.13
  368.9 2.1 copy-start.14
  462.7 1.3 copy-start
  462.8 1.3 copy-start.1
  462.8 1.3 copy-start.2
  462.8 1.3 copy-start.3
  462.8 1.3 copy-start.4
  462.8 1.4 copy-start.6
  462.8 1.4 copy-start.7
  463.4 2.9 copy-start.5
  463.4 16.1 %copy-start.8 = (s32[16]{0:T(128)S(1)}, s32[16]{0:T(128)}, u32[]{:S(2)}) copy-start(s32[16]{0:T(128)} %param.21) | copy-start | bytes 196
  470.8 8.3 %collective-permute-start.2 = (f32[4]{0:T(128)S(1)}, f32[4]{0:T(128)S(1)}, u32[]{:S(2)}, u32[]{:S(2)}) collective-permute-start(f32[4]{0:T(128)S(1)} %pad_maximum_fusion.2), channel_id=1, source_target_pairs={{0,96},{32,0},{64,32},{96,64},{1,97},{33,1},{65,33},{97,65},{2,98}... | collective-permute-start | bytes 56 | tf_op jit(solution)/shard_map/ppermute | solution.py:85
  473.5 5.8 %collective-permute-start.1 = (f32[4]{0:T(128)S(1)}, f32[4]{0:T(128)S(1)}, u32[]{:S(2)}, u32[]{:S(2)}) collective-permute-start(f32[4]{0:T(128)S(1)} %pad_maximum_fusion.2), channel_id=1, source_target_pairs={{0,64},{32,96},{64,0},{96,32},{1,65},{33,97},{65,1},{97,33},{2,66}... | collective-permute-start | bytes 56 | tf_op jit(solution)/shard_map/ppermute | solution.py:85
  473.9 5.5 %collective-permute-start = (f32[4]{0:T(128)S(1)}, f32[4]{0:T(128)S(1)}, u32[]{:S(2)}, u32[]{:S(2)}) collective-permute-start(f32[4]{0:T(128)S(1)} %pad_maximum_fusion.2), channel_id=1, source_target_pairs={{0,32},{32,64},{64,96},{96,0},{1,33},{33,65},{65,97},{97,1},{2,34}... | collective-permute-start | bytes 56 | tf_op jit(solution)/shard_map/ppermute | solution.py:85
Sparse Core Ops, SparseCore 0:
  104.1 76.7 all-gather.10
  205.9 70.4 all-gather.16
  303.4 69.4 all-gather.18
  375.0 41.7 all-gather.12
  419.0 41.8 all-gather.14
